TPU v7x, 512 devices: a whole 4x8x8 slice. The times are simulated.
512 devices in a mesh: dp: 4 (over x), shard: 128 (over z, y, core).
Axes of the slice: x: 4, y: 8, z: 8, core: 2. Of those that a mesh axis runs over, the one named last changes fastest.
Arguments:
- grad_parts: float32 [4, 1024, 16384], P('dp', None, 'shard'), may hold values from -0.3 to 0.3
- owner: int32 [1024], replicated, may hold values from 0 to 127, as said below
- master: float32 [4, 128, 4, 128, 128], P('dp', 'shard'), may hold values from -6 to 6
- first_moment: float32 [4, 128, 4, 128, 128], P('dp', 'shard'), may hold values from -0.12 to 0.12
- second_moment: float32 [4, 128, 4, 128, 128], P('dp', 'shard'), may hold values from 0.0001 to 0.001
- left_stat: float32 [4, 128, 4, 128, 128], P('dp', 'shard'), may hold values from -0.0062992126 to 10
- right_stat: float32 [4, 128, 4, 128, 128], P('dp', 'shard'), may hold values from -0.0062992126 to 10
- left_basis: float32 [4, 128, 4, 128, 128], P('dp', 'shard'), may hold values from -0.079549513 to 1.0795495
- right_basis: float32 [4, 128, 4, 128, 128], P('dp', 'shard'), may hold values from -0.079549513 to 1.0795495
Outputs:
- new_params: bfloat16 [1024, 16384], P(None, 'shard')
- master_out: float32 [4, 128, 4, 128, 128], P('dp', 'shard')
- first_out: float32 [4, 128, 4, 128, 128], P('dp', 'shard')
- second_out: float32 [4, 128, 4, 128, 128], P('dp', 'shard')
- left_stat_out: float32 [4, 128, 4, 128, 128], P('dp', 'shard')
- right_stat_out: float32 [4, 128, 4, 128, 128], P('dp', 'shard')
- left_basis_out: float32 [4, 128, 4, 128, 128], P('dp', 'shard')
- right_basis_out: float32 [4, 128, 4, 128, 128], P('dp', 'shard')
Inputs may be any that keep to these rules, and one draw needn't show every extreme that they name: In each group of 256 consecutive tiles no owner index holds more than 4 tiles, and some owner holds exactly 4.
All inputs are finite; a program needn't handle non-finite values.
Results may differ from a plain program's by a relative error of at most 0.001.
Values may be sent and summed in bfloat16 or wider, within the bound.
No kernel may reach another device: no remote copies, remote signals or barrier semaphores. Data moves between devices by JAX's collectives and lax.ppermute only.
A program may use at most 64 MiB of HBM per device.

v0:
```python
import jax
import jax.numpy as jnp
from jax import lax
from jax.sharding import PartitionSpec as P

NS_STEPS = 10
beta_one = 0.9
beta_two = 0.95
stat_decay = 0.95
learn_rate = 0.05
weight_decay = 0.01
adam_eps = 1e-08
highest = lax.Precision.HIGHEST


def product(form, left, right):
    return jnp.einsum(form, left, right, precision=highest)


def slot_index(owners, shards):
    matches = (owners[..., None] == jnp.arange(shards, dtype=jnp.int32)).astype(jnp.int32)
    running = jnp.cumsum(matches, axis=1)
    return jnp.sum(matches * running, axis=-1) - 1


def orthogonal(pending):
    iterate = pending * lax.rsqrt(jnp.sum(pending * pending, axis=(1, 2), keepdims=True) + 1e-06)
    for step in range(NS_STEPS):
        gram = product("nik,njk->nij", iterate, iterate)
        iterate = 1.5 * iterate - 0.5 * product("nij,njk->nik", gram, iterate)
    return iterate


def soap_update(gradient, master, first, second, lstat, rstat, lbasis, rbasis):
    first_new = beta_one * first + (1.0 - beta_one) * gradient
    grad_rot = product("nik,nkl->nil", product("nji,njk->nik", lbasis, gradient), rbasis)
    first_rot = product("nik,nkl->nil", product("nji,njk->nik", lbasis, first_new), rbasis)
    second_new = beta_two * second + (1.0 - beta_two) * grad_rot * grad_rot
    normed = first_rot / (jnp.sqrt(second_new) + adam_eps)
    update = product("nik,nlk->nil", product("nij,njk->nik", lbasis, normed), rbasis)
    master_new = master - learn_rate * (update + weight_decay * master)
    lstat_new = stat_decay * lstat + (1.0 - stat_decay) * product(
        "nik,njk->nij", gradient, gradient
    )
    rstat_new = stat_decay * rstat + (1.0 - stat_decay) * product(
        "nki,nkj->nij", gradient, gradient
    )
    lbasis_new = orthogonal(product("nij,njk->nik", lstat_new, lbasis))
    rbasis_new = orthogonal(product("nij,njk->nik", rstat_new, rbasis))
    return (master_new, first_new, second_new, lstat_new, rstat_new, lbasis_new, rbasis_new)


def body(
    grad_parts,
    owner,
    master,
    first_moment,
    second_moment,
    left_stat,
    right_stat,
    left_basis,
    right_basis,
):
    shards = lax.axis_size("shard")
    groups = lax.axis_size("dp")
    my_group = lax.axis_index("dp")
    capacity = master.shape[2]
    block_size = master.shape[4]
    piece_len = grad_parts.shape[2]
    tile_count = owner.shape[0]
    per_group = tile_count // groups
    owners = owner.reshape(groups, per_group)
    place_index = slot_index(owners, shards) * shards + owners
    own_place = lax.dynamic_index_in_dim(place_index, my_group, 0, keepdims=False)
    summed = lax.psum_scatter(grad_parts, "dp", scatter_dimension=1, tiled=True)
    outgoing = jnp.zeros((capacity * shards, piece_len), jnp.float32)
    outgoing = outgoing.at[own_place].set(summed[0])
    outgoing = outgoing.reshape(capacity, shards, piece_len)
    incoming = lax.all_to_all(outgoing, "shard", split_axis=1, concat_axis=1, tiled=True)

    def as_tiles(array):
        return array.reshape(capacity, block_size, block_size)

    results = soap_update(
        incoming,
        as_tiles(master),
        as_tiles(first_moment),
        as_tiles(second_moment),
        as_tiles(left_stat),
        as_tiles(right_stat),
        as_tiles(left_basis),
        as_tiles(right_basis),
    )
    shaped = [item.reshape(1, 1, capacity, block_size, block_size) for item in results]
    weights = results[0].astype(jnp.bfloat16)
    returned = lax.all_to_all(weights, "shard", split_axis=1, concat_axis=1, tiled=True)
    returned = returned.reshape(capacity * shards, piece_len)
    own_rows = returned[own_place]
    new_params = lax.all_gather(own_rows, "dp", axis=0, tiled=True)
    return (new_params, shaped[0], shaped[1], shaped[2], shaped[3], shaped[4], shaped[5], shaped[6])


def solution(mesh):
    placed = (
        P("dp", None, "shard"),
        P(),
        P("dp", "shard", None, None, None),
        P("dp", "shard", None, None, None),
        P("dp", "shard", None, None, None),
        P("dp", "shard", None, None, None),
        P("dp", "shard", None, None, None),
        P("dp", "shard", None, None, None),
        P("dp", "shard", None, None, None),
    )
    return jax.shard_map(
        body,
        mesh=mesh,
        in_specs=placed,
        out_specs=(
            P(None, "shard"),
            P("dp", "shard", None, None, None),
            P("dp", "shard", None, None, None),
            P("dp", "shard", None, None, None),
            P("dp", "shard", None, None, None),
            P("dp", "shard", None, None, None),
            P("dp", "shard", None, None, None),
            P("dp", "shard", None, None, None),
        ),
        check_vma=False,
    )
```

profile of v0, /device:TPU:8, one launch (start us, length us, event | category | flops | bytes accessed | tf_op | source)
XLA Modules:
  0.0 143.0 jit_solution(8679170944378737934)
XLA Ops:
  7.2 0.7 reduce-scatter.2.cloned.1.call-update
  7.9 0.7 copy-done.10
  8.8 0.9 fusion.26
  10.3 31.9 %reduce-scatter.2.cloned.1.call-done = f32[1,256,128]{2,1,0:T(8,128)} async-done(((f32[1,1024,128]{2,1,0:T(8,128)}), f32[1,256,128]{2,1,0:T(8,128)}) %reduce-scatter.2.cloned.1.call-update) | async-done | bytes 131088 | tf_op jit(solution)/shard_map/reduce_scatter | solution.py:75
  42.2 1.6 %scatter_custom_fusion = f32[512,128]{1,0:T(8,128)S(1)} fusion(s32[256]{0:T(256)S(1)} %bitcast.159, f32[1,256,128]{2,1,0:T(8,128)} %reduce-scatter.2.cloned.1.call-done, f32[]{:T(128)} %constant.18.clone.1), kind=kCustom, calls=%fused_computation.91 | custom fusion | bytes 393220 | tf_op jit(solution)/shard_map/scatter | solution.py:77
  43.8 0.9 copy.40
  44.7 14.5 %all-to-all-start = ((f32[4,128,128]{2,0,1:T(4,128)}), f32[4,128,128]{2,0,1:T(4,128)S(1)}, u32[]{:S(2)}, u32[]{:S(2)}) async-start(f32[4,128,128]{2,0,1:T(4,128)} %copy.40), calls=%async_computation.1 | async-start | bytes 524288 | tf_op jit(solution)/shard_map/all_to_all | solution.py:79
  59.2 14.5 %all-to-all-done = f32[4,128,128]{2,0,1:T(4,128)S(1)} async-done(((f32[4,128,128]{2,0,1:T(4,128)}), f32[4,128,128]{2,0,1:T(4,128)S(1)}, u32[]{:S(2)}, u32[]{:S(2)}) %all-to-all-start) | async-done | bytes 262176 | tf_op jit(solution)/shard_map/all_to_all | solution.py:79
  74.2 0.5 multiply_reduce_fusion
  74.9 0.8 fusion.51
  75.7 0.4 fusion.10
  76.1 0.7 fusion.76
  77.2 0.7 fusion.77
  78.3 0.7 fusion.78
  79.4 0.7 fusion.79
  80.4 0.7 fusion.80
  81.5 0.7 fusion.81
  82.6 0.7 fusion.82
  83.7 0.7 fusion.83
  84.8 0.7 fusion.84
  85.7 0.6 fusion.43
  86.7 0.7 fusion.23
  87.3 0.5 multiply_reduce_fusion.1
  88.0 0.8 fusion.54
  88.8 0.4 fusion.21
  89.2 0.7 fusion.67
  90.3 0.8 fusion.68
  91.6 0.7 fusion.69
  92.7 0.7 fusion.70
  93.8 0.7 fusion.71
  94.8 0.7 fusion.72
  95.9 0.7 fusion.73
  97.0 0.7 fusion.74
  98.1 0.7 fusion.75
  99.0 0.6 fusion.45
  99.9 0.4 fusion.29
  100.4 0.4 convolution_divide_fusion
  101.4 0.6 copy-done.9
  102.0 1.4 fusion.66
  103.4 0.8 copy.47
  104.1 6.1 %all-to-all-start.1 = ((bf16[4,128,128]{2,0,1:T(4,128)(2,1)}), bf16[4,128,128]{2,0,1:T(4,128)(2,1)S(1)}, u32[]{:S(2)}, u32[]{:S(2)}) async-start(bf16[4,128,128]{2,0,1:T(4,128)(2,1)} %copy.47), calls=%async_computation.2 | async-start | bytes 262144 | tf_op jit(solution)/shard_map/all_to_all | solution.py:96
  110.2 0.7 copy.53
  111.0 1.1 fusion.1
  112.1 1.1 fusion.12
  113.2 9.1 %all-to-all-done.1 = bf16[4,128,128]{2,0,1:T(4,128)(2,1)S(1)} async-done(((bf16[4,128,128]{2,0,1:T(4,128)(2,1)}), bf16[4,128,128]{2,0,1:T(4,128)(2,1)S(1)}, u32[]{:S(2)}, u32[]{:S(2)}) %all-to-all-start.1) | async-done | bytes 131104 | tf_op jit(solution)/shard_map/all_to_all | solution.py:96
  122.3 0.9 gather_fusion
  123.2 12.3 %all-gather = bf16[1024,128]{1,0:T(8,128)(2,1)S(1)} all-gather(bf16[256,128]{1,0:T(8,128)(2,1)S(1)} %gather_fusion), channel_id=2, replica_groups=mesh['dp'=4,'shard'=128] {'dp'}, dimensions={0}, use_global_device_ids=true | all-gather | bytes 327680 | tf_op jit(solution)/shard_map/all_gather | solution.py:99
  135.5 0.7 copy.69
  (55 shorter events, 10.3 us)
Async XLA Ops:
  7.2 67.0 %copy-start = (f32[1,1,4,128,128]{4,3,2,1,0:T(8,128)S(1)}, f32[1,1,4,128,128]{4,3,2,1,0:T(8,128)}, u32[]{:S(2)}) copy-start(f32[1,1,4,128,128]{4,3,2,1,0:T(8,128)} %param.17) | copy-start | bytes 786436
  7.2 35.0 %reduce-scatter.2.cloned.1.call-start = ((), (), s32[]{:S(2)}) async-start(), calls=%async_computation.3 | async-start | bytes 655360 | tf_op jit(solution)/shard_map/reduce_scatter | solution.py:75
  7.9 0.7 copy-start.10
  44.6 14.5 %copy-start.6 = (f32[1,1,4,128,128]{4,3,2,1,0:T(8,128)S(1)}, f32[1,1,4,128,128]{4,3,2,1,0:T(8,128)}, u32[]{:S(2)}) copy-start(f32[1,1,4,128,128]{4,3,2,1,0:T(8,128)} %param.12) | copy-start | bytes 786436
  44.7 29.0 %all-to-all-start = ((f32[4,128,128]{2,0,1:T(4,128)}), f32[4,128,128]{2,0,1:T(4,128)S(1)}, u32[]{:S(2)}, u32[]{:S(2)}) async-start(f32[4,128,128]{2,0,1:T(4,128)} %copy.40), calls=%async_computation.1 | async-start | bytes 524288 | tf_op jit(solution)/shard_map/all_to_all | solution.py:79
  59.2 14.6 %copy-start.7 = (f32[1,1,4,128,128]{4,3,2,1,0:T(8,128)S(1)}, f32[1,1,4,128,128]{4,3,2,1,0:T(8,128)}, u32[]{:S(2)}) copy-start(f32[1,1,4,128,128]{4,3,2,1,0:T(8,128)} %param.15) | copy-start | bytes 786436
  74.2 0.7 copy-start.3
  84.8 1.0 copy-start.1
  85.7 0.9 copy-start.5
  87.3 0.7 copy-start.2
  99.0 1.0 copy-start.8
  100.3 0.7 copy-start.4
  101.1 0.9 copy-start.9
  104.1 18.2 %all-to-all-start.1 = ((bf16[4,128,128]{2,0,1:T(4,128)(2,1)}), bf16[4,128,128]{2,0,1:T(4,128)(2,1)S(1)}, u32[]{:S(2)}, u32[]{:S(2)}) async-start(bf16[4,128,128]{2,0,1:T(4,128)(2,1)} %copy.47), calls=%async_computation.2 | async-start | bytes 262144 | tf_op jit(solution)/shard_map/all_to_all | solution.py:96
Sparse Core Ops, SparseCore 0:
  10.8 31.2 reduce-scatter.1
where the time goes:
time: 143 us
  waiting for transfers between devices  56.1 us (39%)
  matrix products  28.9 us (20%)
  starting transfers between devices  20.6 us (14%)
  between operations  14.6 us (10%)
  blocking collectives  12.3 us (9%)
  local copies, waits for them, and re-layouts  8.78 us (6%)
  other arithmetic  1.75 us (1%)
    reduce_scatter x1, waiting for transfers between devices, body(): summed = lax.psum_scatter(grad_parts, 'dp', scatter_dimension=1, tiled=True)  31.9 us
    dot_general x50, matrix products, product(): return jnp.einsum(form, left, right, precision=highest)  28.9 us
    all_to_all x1, waiting for transfers between devices, body(): lax.all_to_all(outgoing, 'shard', split_axis=1, concat_axis=1, tiled=True)  14.5 us
    all_to_all x1, starting transfers between devices, body(): lax.all_to_all(outgoing, 'shard', split_axis=1, concat_axis=1, tiled=True)  14.5 us
    all_gather x1, blocking collectives, body(): new_params = lax.all_gather(own_rows, 'dp', axis=0, tiled=True)  12.3 us
    all_to_all x1, waiting for transfers between devices, body(): lax.all_to_all(weights, 'shard', split_axis=1, concat_axis=1, tiled=True)  9.13 us
    all_to_all x1, starting transfers between devices, body(): lax.all_to_all(weights, 'shard', split_axis=1, concat_axis=1, tiled=True)  6.1 us
    unnamed x24, local copies, waits for them, and re-layouts  4.36 us
  transfers between devices with their start and end apart: 3, of which 3 were waited for; matrix products, arithmetic and copies ran while one was open for 3% of the time, Pallas kernels for 0%

commit v1 on v0

--- a/solution.py
+++ b/solution.py
@@ -61,6 +61,23 @@
     left_basis,
     right_basis,
 ):
+
+    def tables_obtain(arr):
+        parts_n = jax.lax.axis_size("dp")
+        block_list = [(j0, (j0 + 1) % parts_n) for j0 in range(parts_n)]
+        trail = [(j0, (j0 - 1) % parts_n) for j0 in range(parts_n)]
+        top, latest = ([arr], [arr])
+        for _ in range(parts_n // 2):
+            local_next = jax.lax.ppermute(top[-1], "dp", block_list)
+            top.append(local_next)
+        for _ in [*range((parts_n - 1) // 2)]:
+            finding = jax.lax.ppermute(latest[-1], "dp", trail)
+            latest.append(finding)
+        moved = jnp.concatenate([*top[::-1], *latest[1:]], 0)
+        step_out = jax.lax.axis_index("dp")
+        state_now = jnp.roll(moved, (step_out - parts_n // 2) * arr.shape[0], 0)
+        return state_now
+
     shards = lax.axis_size("shard")
     groups = lax.axis_size("dp")
     my_group = lax.axis_index("dp")
@@ -96,7 +113,7 @@
     returned = lax.all_to_all(weights, "shard", split_axis=1, concat_axis=1, tiled=True)
     returned = returned.reshape(capacity * shards, piece_len)
     own_rows = returned[own_place]
-    new_params = lax.all_gather(own_rows, "dp", axis=0, tiled=True)
+    new_params = tables_obtain(own_rows)
     return (new_params, shaped[0], shaped[1], shaped[2], shaped[3], shaped[4], shaped[5], shaped[6])
 
 

time: 143 us -> 139 us (0.972)
  the two profiles are of different devices: /device:TPU:8 before, /device:TPU:6 now
where the time goes in v1:
time: 139 us; the launch traced here: 138 us
  waiting for transfers between devices  52.5 us (38%)
  starting transfers between devices  32.3 us (23%)
  matrix products  28.9 us (21%)
  between operations  14.7 us (11%)
  local copies, waits for them, and re-layouts  7.92 us (6%)
  other arithmetic  1.74 us (1%)
    reduce_scatter x1, waiting for transfers between devices, body(): summed = lax.psum_scatter(grad_parts, 'dp', scatter_dimension=1, tiled=True)  31.1 us
    dot_general x50, matrix products, product(): return jnp.einsum(form, left, right, precision=highest)  28.9 us
    all_to_all x1, waiting for transfers between devices, body(): lax.all_to_all(outgoing, 'shard', split_axis=1, concat_axis=1, tiled=True)  14.6 us
    all_to_all x1, starting transfers between devices, body(): lax.all_to_all(outgoing, 'shard', split_axis=1, concat_axis=1, tiled=True)  14.1 us
    ppermute x2, starting transfers between devices, tables_obtain(): local_next = jax.lax.ppermute(top[-1], 'dp', block_list)  9.94 us
    all_to_all x1, starting transfers between devices, body(): lax.all_to_all(weights, 'shard', split_axis=1, concat_axis=1, tiled=True)  6.35 us
    ppermute x1, waiting for transfers between devices, tables_obtain(): finding = jax.lax.ppermute(latest[-1], 'dp', trail)  5.38 us
  transfers between devices with their start and end apart: 6, of which 4 were waited for; matrix products, arithmetic and copies ran while one was open for 20% of the time, Pallas kernels for 0%

profile of v1, /device:TPU:6, one launch (start us, length us, event | category | flops | bytes accessed | tf_op | source)
XLA Modules:
  0.0 138.1 jit_solution(15841297133683559648)
XLA Ops:
  7.2 0.7 reduce-scatter.2.cloned.1.call-update
  8.1 0.9 fusion.26
  9.7 31.1 %reduce-scatter.2.cloned.1.call-done = f32[1,256,128]{2,1,0:T(8,128)} async-done(((f32[1,1024,128]{2,1,0:T(8,128)}), f32[1,256,128]{2,1,0:T(8,128)}) %reduce-scatter.2.cloned.1.call-update) | async-done | bytes 131088 | tf_op jit(solution)/shard_map/reduce_scatter | solution.py:92
  40.7 1.6 %scatter_custom_fusion = f32[512,128]{1,0:T(8,128)S(1)} fusion(s32[256]{0:T(256)S(1)} %bitcast.159, f32[1,256,128]{2,1,0:T(8,128)} %reduce-scatter.2.cloned.1.call-done, f32[]{:T(128)} %constant.26.clone.1), kind=kCustom, calls=%fused_computation.91 | custom fusion | bytes 393220 | tf_op jit(solution)/shard_map/scatter | solution.py:94
  42.3 0.9 copy.40
  43.2 14.1 %all-to-all-start = ((f32[4,128,128]{2,0,1:T(4,128)}), f32[4,128,128]{2,0,1:T(4,128)S(1)}, u32[]{:S(2)}, u32[]{:S(2)}) async-start(f32[4,128,128]{2,0,1:T(4,128)} %copy.40), calls=%async_computation.1 | async-start | bytes 524288 | tf_op jit(solution)/shard_map/all_to_all | solution.py:96
  57.4 14.6 %all-to-all-done = f32[4,128,128]{2,0,1:T(4,128)S(1)} async-done(((f32[4,128,128]{2,0,1:T(4,128)}), f32[4,128,128]{2,0,1:T(4,128)S(1)}, u32[]{:S(2)}, u32[]{:S(2)}) %all-to-all-start) | async-done | bytes 262176 | tf_op jit(solution)/shard_map/all_to_all | solution.py:96
  72.3 0.6 fusion.45
  73.0 0.6 fusion.43
  75.5 0.6 copy-done.8
  76.0 1.4 %fusion.66 = (bf16[4,128,128]{2,1,0:T(8,128)(2,1)S(1)}, f32[4,128,128]{2,1,0:T(8,128)}) fusion(f32[4,128,128]{1,2,0:T(8,128)S(1)} %fusion.41, f32[1,1,4,128,128]{4,3,2,1,0:T(8,128)S(1)} %copy-done, f32[1,1,4,128,128]{4,3,2,1,0:T(8,128)S(1)} %copy-done.8), kind=kOutput, calls=%fused_computation.116 | convolution fusion | flops 100990976 | bytes 1179648 | tf_op jit(solution)/shard_map/nik,nlk->nil/dot_general | solution.py:17
  77.4 0.8 copy.47
  78.2 6.4 %all-to-all-start.1 = ((bf16[4,128,128]{2,0,1:T(4,128)(2,1)}), bf16[4,128,128]{2,0,1:T(4,128)(2,1)S(1)}, u32[]{:S(2)}, u32[]{:S(2)}) async-start(bf16[4,128,128]{2,0,1:T(4,128)(2,1)} %copy.47), calls=%async_computation.2 | async-start | bytes 262144 | tf_op jit(solution)/shard_map/all_to_all | solution.py:113
  84.5 0.7 fusion.23
  85.2 0.5 multiply_reduce_fusion.1
  85.9 0.8 fusion.54
  86.7 0.4 fusion.21
  87.1 0.7 fusion.67
  88.2 0.7 fusion.68
  89.3 0.7 fusion.69
  90.4 0.7 fusion.70
  91.4 0.7 fusion.71
  92.5 0.7 fusion.72
  93.6 0.7 fusion.73
  94.7 0.7 fusion.74
  95.8 0.7 fusion.75
  97.1 0.5 multiply_reduce_fusion
  97.8 0.8 fusion.51
  98.6 0.4 fusion.10
  99.0 0.7 fusion.76
  100.1 0.7 fusion.77
  101.2 0.9 fusion.78
  102.5 0.7 fusion.79
  103.6 0.7 fusion.80
  104.6 0.7 fusion.81
  105.7 0.7 fusion.82
  106.8 0.7 fusion.83
  107.9 0.7 fusion.84
  108.6 0.9 gather_fusion
  109.4 4.5 %collective-permute-start = (bf16[256,128]{1,0:T(8,128)(2,1)S(1)}, bf16[256,128]{1,0:T(8,128)(2,1)S(1)}, u32[]{:S(2)}, u32[]{:S(2)}) collective-permute-start(bf16[256,128]{1,0:T(8,128)(2,1)S(1)} %gather_fusion), channel_id=1, source_target_pairs={{0,128},{128,256},{256,384},{384,0},{1,129},{129,257},{257,385},{3... | collective-permute-start | bytes 196616 | tf_op jit(solution)/shard_map/ppermute | solution.py:71
  113.9 1.1 fusion.12
  115.0 0.8 collective-permute-done
  115.8 5.5 %collective-permute-start.1 = (bf16[256,128]{1,0:T(8,128)(2,1)S(1)}, bf16[256,128]{1,0:T(8,128)(2,1)S(1)}, u32[]{:S(2)}, u32[]{:S(2)}) collective-permute-start(bf16[256,128]{1,0:T(8,128)(2,1)S(1)} %collective-permute-done), channel_id=1, source_target_pairs={{0,128},{128,256},{256,384},{384,0},{1,129},{129,257},{257,385},{3... | collective-permute-start | bytes 196616 | tf_op jit(solution)/shard_map/ppermute | solution.py:71
  121.3 1.1 fusion.1
  122.4 0.7 copy.53
  123.1 1.9 %collective-permute-start.2 = (bf16[256,128]{1,0:T(8,128)(2,1)S(1)}, bf16[256,128]{1,0:T(8,128)(2,1)S(1)}, u32[]{:S(2)}, u32[]{:S(2)}) collective-permute-start(bf16[256,128]{1,0:T(8,128)(2,1)S(1)} %gather_fusion), channel_id=1, source_target_pairs={{0,384},{128,0},{256,128},{384,256},{1,385},{129,1},{257,129},{385... | collective-permute-start | bytes 196616 | tf_op jit(solution)/shard_map/ppermute | solution.py:74
  125.1 5.4 %collective-permute-done.2 = bf16[256,128]{1,0:T(8,128)(2,1)S(1)} collective-permute-done((bf16[256,128]{1,0:T(8,128)(2,1)S(1)}, bf16[256,128]{1,0:T(8,128)(2,1)S(1)}, u32[]{:S(2)}, u32[]{:S(2)}) %collective-permute-start.2) | collective-permute-done | bytes 65568 | tf_op jit(solution)/shard_map/ppermute | solution.py:74
  130.5 0.7 constant_dynamic-slice_fusion
  (68 shorter events, 10.9 us)
Async XLA Ops:
  7.2 66.4 %copy-start = (f32[1,1,4,128,128]{4,3,2,1,0:T(8,128)S(1)}, f32[1,1,4,128,128]{4,3,2,1,0:T(8,128)}, u32[]{:S(2)}) copy-start(f32[1,1,4,128,128]{4,3,2,1,0:T(8,128)} %param.17) | copy-start | bytes 786436
  7.2 33.5 %reduce-scatter.2.cloned.1.call-start = ((), (), s32[]{:S(2)}) async-start(), calls=%async_computation.3 | async-start | bytes 655360 | tf_op jit(solution)/shard_map/reduce_scatter | solution.py:92
  7.2 0.7 copy-start.10
  43.2 14.1 %copy-start.6 = (f32[1,1,4,128,128]{4,3,2,1,0:T(8,128)S(1)}, f32[1,1,4,128,128]{4,3,2,1,0:T(8,128)}, u32[]{:S(2)}) copy-start(f32[1,1,4,128,128]{4,3,2,1,0:T(8,128)} %param.12) | copy-start | bytes 786436
  43.2 28.8 %all-to-all-start = ((f32[4,128,128]{2,0,1:T(4,128)}), f32[4,128,128]{2,0,1:T(4,128)S(1)}, u32[]{:S(2)}, u32[]{:S(2)}) async-start(f32[4,128,128]{2,0,1:T(4,128)} %copy.40), calls=%async_computation.1 | async-start | bytes 524288 | tf_op jit(solution)/shard_map/all_to_all | solution.py:96
  57.4 14.9 %copy-start.1 = (f32[1,1,4,128,128]{4,3,2,1,0:T(8,128)S(1)}, f32[1,1,4,128,128]{4,3,2,1,0:T(8,128)}, u32[]{:S(2)}) copy-start(f32[1,1,4,128,128]{4,3,2,1,0:T(8,128)} %param.16) | copy-start | bytes 786436
  73.0 1.0 copy-start.7
  74.4 0.7 copy-start.3
  75.1 0.9 copy-start.8
  77.4 7.1 %copy-start.5 = (f32[1,1,4,128,128]{4,3,2,1,0:T(8,128)S(1)}, f32[1,1,4,128,128]{4,3,2,1,0:T(8,128)}, u32[]{:S(2)}) copy-start(f32[1,1,4,128,128]{4,3,2,1,0:T(8,128)} %param.14) | copy-start | bytes 786436
  78.2 30.4 %all-to-all-start.1 = ((bf16[4,128,128]{2,0,1:T(4,128)(2,1)}), bf16[4,128,128]{2,0,1:T(4,128)(2,1)S(1)}, u32[]{:S(2)}, u32[]{:S(2)}) async-start(bf16[4,128,128]{2,0,1:T(4,128)(2,1)} %copy.47), calls=%async_computation.2 | async-start | bytes 262144 | tf_op jit(solution)/shard_map/all_to_all | solution.py:113
  85.2 0.7 copy-start.2
  95.8 1.0 copy-start.9
  97.1 0.7 copy-start.4
  109.4 6.4 %collective-permute-start = (bf16[256,128]{1,0:T(8,128)(2,1)S(1)}, bf16[256,128]{1,0:T(8,128)(2,1)S(1)}, u32[]{:S(2)}, u32[]{:S(2)}) collective-permute-start(bf16[256,128]{1,0:T(8,128)(2,1)S(1)} %gather_fusion), channel_id=1, source_target_pairs={{0,128},{128,256},{256,384},{384,0},{1,129},{129,257},{257,385},{3... | collective-permute-start | bytes 196616 | tf_op jit(solution)/shard_map/ppermute | solution.py:71
  115.8 9.2 %collective-permute-start.1 = (bf16[256,128]{1,0:T(8,128)(2,1)S(1)}, bf16[256,128]{1,0:T(8,128)(2,1)S(1)}, u32[]{:S(2)}, u32[]{:S(2)}) collective-permute-start(bf16[256,128]{1,0:T(8,128)(2,1)S(1)} %collective-permute-done), channel_id=1, source_target_pairs={{0,128},{128,256},{256,384},{384,0},{1,129},{129,257},{257,385},{3... | collective-permute-start | bytes 196616 | tf_op jit(solution)/shard_map/ppermute | solution.py:71
  123.1 7.4 %collective-permute-start.2 = (bf16[256,128]{1,0:T(8,128)(2,1)S(1)}, bf16[256,128]{1,0:T(8,128)(2,1)S(1)}, u32[]{:S(2)}, u32[]{:S(2)}) collective-permute-start(bf16[256,128]{1,0:T(8,128)(2,1)S(1)} %gather_fusion), channel_id=1, source_target_pairs={{0,384},{128,0},{256,128},{384,256},{1,385},{129,1},{257,129},{385... | collective-permute-start | bytes 196616 | tf_op jit(solution)/shard_map/ppermute | solution.py:74
Sparse Core Ops, SparseCore 0:
  10.8 29.8 reduce-scatter.1
